TPU v7x, 256 devices: a whole 4x4x8 slice. The times are simulated.
256 devices in a mesh: dp: 4 (over y), section: 16 (over z, x_lo), tensor: 4 (over x_hi, core).
Axes of the slice: x: 4 (x_hi: 2, x_lo: 2; x = x_hi * 2 + x_lo), y: 4, z: 8, core: 2. Of those that a mesh axis runs over, the one named last changes fastest.
Arguments:
- saved_input: bfloat16 [16, 2, 512, 8192], P('section', None, ('dp', 'tensor')), may hold values from -6 to 6
- kv_grad: bfloat16 [16, 2, 512, 2048], P('section', None, 'dp', 'tensor'), may hold values from -1.5 to 1.5
- kv_weight: bfloat16 [16, 8192, 2048], P('section', 'dp', 'tensor'), may hold values from -0.0625 to 0.0625
- norm_gain: bfloat16 [16, 8192], P('section'), may hold values from 0.5 to 1.5
- top_grad: bfloat16 [2, 512, 8192], P(None, ('dp', 'tensor')), may hold values from -1.5 to 1.5
- noise_salt: int32 [1], replicated, may hold values from 0 to 1073741823
- step_counter: int32 [1], replicated, may hold values from 0 to 999999
Outputs:
- input_grads: bfloat16 [16, 2, 512, 8192], P('section', None, ('dp', 'tensor'))
- weight_grads: float32 [16, 8192, 2048], P('section', 'dp', 'tensor')
All inputs are finite; a program needn't handle non-finite values.
Results may differ from a plain program's by a relative error of at most 0.012.
Values may be sent and summed in bfloat16 or wider, within the bound.
No kernel may reach another device: no remote copies, remote signals or barrier semaphores. Data moves between devices by JAX's collectives and lax.ppermute only.
A program may use at most 128 MiB of HBM per device.

v0:
```python
import jax
import jax.numpy as jnp
from jax import lax
from jax.sharding import PartitionSpec as P


def mix_bits(salt, counter, layer, group, index):
    h = (
        index * jnp.int32(-1640531535)
        + salt * jnp.int32(374761393)
        + counter * jnp.int32(668265263)
    )
    h = h + layer * jnp.int32(-1028477379) + group * jnp.int32(1274126177)
    h = h ^ lax.shift_right_logical(h, jnp.int32(16))
    h = h * jnp.int32(2146121005)
    h = h ^ lax.shift_right_logical(h, jnp.int32(15))
    h = h * jnp.int32(-2073254261)
    h = h ^ lax.shift_right_logical(h, jnp.int32(16))
    return lax.shift_right_logical(h, jnp.int32(8)).astype(jnp.float32) * (1.0 / 16777216.0)


def dither(term, salt, counter, layer, group, index):
    noise = mix_bits(salt, counter, layer, group, index)
    moved = term * (1.0 + (noise - 0.5) * 0.5)
    return lax.optimization_barrier(moved.astype(jnp.bfloat16)).astype(jnp.float32)


def later_sum(branch_path):
    n_sec = lax.axis_size("section")
    m, t, d = branch_path.shape
    chunks = lax.all_to_all(
        branch_path.astype(jnp.bfloat16)[None], "section", 3, 0, tiled=True
    ).astype(jnp.float32)
    acc = jnp.zeros(chunks.shape[1:], jnp.float32)
    outs = [None] * n_sec
    for s in range(n_sec - 1, -1, -1):
        outs[s] = acc
        acc = acc + chunks[s]
    stacked = jnp.stack(outs).astype(jnp.bfloat16)
    back = lax.all_to_all(stacked, "section", 0, 3, tiled=True)
    return back[0].astype(jnp.float32)


def shards(saved_input, kv_grad, kv_weight, norm_gain, top_grad, noise_salt, step_counter):
    salt = noise_salt[0]
    counter = step_counter[0]
    layer = lax.axis_index("section")
    n_dp = lax.axis_size("dp")
    n_t = lax.axis_size("tensor")
    my_p = lax.axis_index("dp")
    my_t = lax.axis_index("tensor")
    cotan = kv_grad[0]
    weight = kv_weight[0]
    rows_p, width_t = weight.shape
    total_cols = width_t * n_t
    mb, tok_dev, d_model = saved_input.shape[1:]
    input_float = saved_input[0].astype(jnp.float32)
    inverse_scale = lax.rsqrt(jnp.mean(input_float * input_float, axis=-1, keepdims=True) + 1e-05)
    centered_input = input_float * inverse_scale
    gain_float = norm_gain[0].astype(jnp.float32)
    normed_values = (centered_input * gain_float).astype(jnp.bfloat16)
    cotan_all = lax.all_gather(cotan, "dp", axis=1, tiled=True)
    part = jnp.einsum("mtk,dk->mtd", cotan_all, weight, preferred_element_type=jnp.float32).astype(
        jnp.bfloat16
    )
    part = part.reshape(mb, n_dp * n_t, tok_dev, rows_p).transpose(1, 0, 2, 3)
    got = lax.all_to_all(part, ("dp", "tensor"), 0, 0, tiled=True)
    got = got.reshape(n_dp, n_t, mb, tok_dev, rows_p).astype(jnp.float32)
    normed_grad = got[:, 0]
    for t in range(1, n_t):
        normed_grad = normed_grad + got[:, t]
    normed_grad = normed_grad.transpose(1, 2, 0, 3).reshape(mb, tok_dev, d_model)
    hidden_gradient = normed_grad * gain_float
    branch_path = inverse_scale * (
        hidden_gradient
        - centered_input * jnp.mean(hidden_gradient * centered_input, axis=-1, keepdims=True)
    )
    later = later_sum(branch_path)
    grad_in = (top_grad.astype(jnp.float32) + branch_path + later).astype(jnp.bfloat16)
    nrm = normed_values.reshape(mb, tok_dev, n_dp, rows_p).transpose(2, 0, 1, 3)
    nrm = lax.all_to_all(nrm, "dp", 0, 0, tiled=True)
    nrm = lax.all_gather(nrm, "tensor", axis=0, tiled=False)
    cot = cotan_all.reshape(mb, n_dp, n_t, tok_dev, width_t)
    terms = jnp.einsum("tpmid,mptik->pdk", nrm, cot, preferred_element_type=jnp.float32)
    row_ids = my_p * jnp.int32(rows_p) + jnp.arange(rows_p, dtype=jnp.int32)
    index = (
        row_ids[:, None] * jnp.int32(total_cols)
        + my_t * jnp.int32(width_t)
        + jnp.arange(width_t, dtype=jnp.int32)[None, :]
    )
    wsum = jnp.zeros((rows_p, width_t), jnp.float32)
    for g in range(n_dp):
        wsum = wsum + dither(terms[g], salt, counter, layer, jnp.int32(g), index)
    return (grad_in[None], wsum[None])


def solution(mesh):
    placed = (
        P("section", None, ("dp", "tensor"), None),
        P("section", None, "dp", "tensor"),
        P("section", "dp", "tensor"),
        P("section", None),
        P(None, ("dp", "tensor"), None),
        P(),
        P(),
    )
    return jax.shard_map(
        shards,
        mesh=mesh,
        in_specs=placed,
        out_specs=(P("section", None, ("dp", "tensor"), None), P("section", "dp", "tensor")),
        check_vma=False,
    )
```

profile of v0, /device:TPU:8, one launch (start us, length us, event | category | flops | bytes accessed | tf_op | source)
XLA Modules:
  0.0 288.4 jit_solution(17948738188843804011)
XLA Ops:
  7.9 30.3 %all-gather.5.cloned.1.call-done = bf16[1,2,512,512]{3,2,1,0:T(8,128)(2,1)} async-done(((bf16[1,2,128,512]{3,2,1,0:T(8,128)(2,1)}), bf16[1,2,512,512]{3,2,1,0:T(8,128)(2,1)}) %all-gather.5.cloned.1.call-update) | async-done | bytes 1048592 | tf_op jit(solution)/shard_map/all_gather | solution.py:62
  38.2 3.6 %convolution_convert_fusion = bf16[2,512,2048]{2,1,0:T(8,128)(2,1)S(1)} fusion(bf16[1,2048,512]{2,1,0:T(8,128)(2,1)S(1)} %copy-done, bf16[1,2,512,512]{3,2,1,0:T(8,128)(2,1)} %all-gather.5.cloned.1.call-done), kind=kOutput, calls=%fused_computation.60 | convolution fusion | flops 2149580800 | bytes 7340032 | tf_op jit(solution)/shard_map/mtk,dk->mtd/dot_general | solution.py:63
  44.1 7.6 %all-to-all-start = ((bf16[16,2,32,2048]{3,2,1,0:T(8,128)(2,1)}), bf16[16,2,32,2048]{3,2,1,0:T(8,128)(2,1)}, u32[]{:S(2)}, u32[]{:S(2)}) async-start(bf16[16,2,32,2048]{3,2,1,0:T(8,128)(2,1)} %bitcast.145), calls=%async_computation | async-start | bytes 8388608 | tf_op jit(solution)/shard_map/all_to_all | solution.py:67
  55.0 47.1 %all-to-all-done = bf16[16,2,32,2048]{3,2,1,0:T(8,128)(2,1)} async-done(((bf16[16,2,32,2048]{3,2,1,0:T(8,128)(2,1)}), bf16[16,2,32,2048]{3,2,1,0:T(8,128)(2,1)}, u32[]{:S(2)}, u32[]{:S(2)}) %all-to-all-start) | async-done | bytes 4194336 | tf_op jit(solution)/shard_map/all_to_all | solution.py:67
  102.0 3.4 %bitcast_convert_fusion = f32[4,4,2,32,2048]{4,3,2,1,0:T(8,128)S(1)} fusion(bf16[16,2,32,2048]{3,2,1,0:T(8,128)(2,1)} %all-to-all-done), kind=kLoop, calls=%fused_computation.121 | loop fusion | flops 2097152 | bytes 12582912 | tf_op jit(solution)/shard_map/convert_element_type | solution.py:68
  105.5 3.0 %multiply_reduce_fusion = (f32[2,32]{1,0:T(2,128)S(1)}, f32[4,1,2,32,2048]{4,3,2,1,0:T(8,128)S(1)}, bf16[4,2,32,2048]{3,2,1,0:T(8,128)(2,1)}) fusion(f32[2,32,4,2048]{3,2,1,0:T(4,128)S(1)} %copy-done.4, f32[2,32]{1,0:T(2,128)S(1)} %add_rsqrt_fusion, f32[4,2048]{1,0:T(4,128)S(1)} %reshape.106, f32[4,4,2,32,2048]{4,3,2,1,0:T(8,128)S(1)} %bitcast_convert_fusion), kind=kLoop, calls=%fused_computation.78 | loop fusion | flops 4718528 | bytes 13664768 | tf_op jit(solution)/shard_map/reduce_sum | solution.py:76
  108.4 5.9 %all-to-all-start.3 = ((bf16[4,2,32,2048]{3,2,1,0:T(8,128)(2,1)}), bf16[4,2,32,2048]{3,2,1,0:T(8,128)(2,1)}, u32[]{:S(2)}, u32[]{:S(2)}) async-start(bf16[4,2,32,2048]{3,2,1,0:T(8,128)(2,1)} %get-tuple-element.20), calls=%async_computation.3 | async-start | bytes 2097152 | tf_op jit(solution)/shard_map/all_to_all | solution.py:81
  117.0 3.6 %reshape.101 = f32[1,2,32,8192]{3,2,1,0:T(8,128)} reshape(f32[2,32,4,2048]{3,2,1,0:T(4,128)} %copy.102) | data formatting | bytes 4194304 | tf_op jit(solution)/shard_map/reshape | solution.py:72
  120.6 3.1 %multiply_convert_fusion.1 = bf16[1,2,32,8192]{3,2,1,0:T(8,128)(2,1)} fusion(f32[1,2,32,8192]{3,2,1,0:T(8,128)} %reshape.101, bf16[1,2,32,8192]{3,2,1,0:T(8,128)(2,1)S(1)} %copy-done.2, f32[2,32]{1,0:T(2,128)S(1)} %broadcast_multiply_fusion, f32[8192]{0:T(1024)S(1)} %bitcast.151, f32[2,32]{1,0:T(2,128)S(1)} %add_rsqrt_fusion), kind=kLoop, calls=%fused_computation.77 | loop fusion | flops 3670016 | bytes 4227584 | tf_op jit(solution)/shard_map/convert_element_type | solution.py:32
  123.7 9.2 %copy.105 = bf16[1,2,32,8192]{2,1,0,3:T(2,128)(2,1)} copy(bf16[1,2,32,8192]{3,2,1,0:T(8,128)(2,1)} %multiply_convert_fusion.1) | data formatting | bytes 2097152 | tf_op jit(solution)/shard_map/convert_element_type | solution.py:32
  132.8 9.9 %reshape.147 = bf16[16,2,16384]{2,1,0:T(2,128)(2,1)} reshape(bf16[8192,1,2,32]{3,2,1,0:T(2,128)(2,1)} %bitcast.143) | data formatting | bytes 2097152
  142.8 7.2 %all-to-all-start.1 = ((bf16[16,2,16384]{2,1,0:T(2,128)(2,1)}), bf16[16,2,16384]{2,1,0:T(2,128)(2,1)}, u32[]{:S(2)}, u32[]{:S(2)}) async-start(bf16[16,2,16384]{2,1,0:T(2,128)(2,1)} %reshape.147), calls=%async_computation.1 | async-start | bytes 2097152 | tf_op jit(solution)/shard_map/all_to_all | solution.py:31
  150.7 27.2 %all-to-all-done.1 = bf16[16,2,16384]{2,1,0:T(2,128)(2,1)} async-done(((bf16[16,2,16384]{2,1,0:T(2,128)(2,1)}), bf16[16,2,16384]{2,1,0:T(2,128)(2,1)}, u32[]{:S(2)}, u32[]{:S(2)}) %all-to-all-start.1) | async-done | bytes 1048608 | tf_op jit(solution)/shard_map/all_to_all | solution.py:31
  177.9 10.0 %reshape.148 = bf16[8192,1,2,32]{3,2,1,0:T(2,128)(2,1)} reshape(bf16[16,2,16384]{2,1,0:T(2,128)(2,1)} %all-to-all-done.1) | data formatting | bytes 2097152
  187.9 9.0 %copy.106 = bf16[1,2,32,8192]{3,2,1,0:T(8,128)(2,1)} copy(bf16[1,2,32,8192]{2,1,0,3:T(2,128)(2,1)} %bitcast.144) | data formatting | bytes 2097152 | tf_op jit(solution)/shard_map/all_to_all | solution.py:31
  211.0 7.5 %stack.3 = bf16[16,2,32,512]{3,0,2,1:T(8,128)(2,1)} concatenate(bf16[1,2,32,512]{3,0,2,1:T(2,128)(2,1)S(1)} %fusion.53, bf16[1,2,32,512]{3,0,2,1:T(2,128)(2,1)S(1)} %copy.122, bf16[1,2,32,512]{3,0,2,1:T(2,128)(2,1)} %copy.123, bf16[1,2,32,512]{3,0,2,1:T(2,128)(2,1)S(1)} %copy.124, bf16[1,2,32,512]{3,0,2,1:T(2,128)(2,1)} %copy.125, bf16[1,2,32,512]{3,0,2,1:T(2,128)(2,1)} %copy.126, ...), dimensions={0} | concatenate | bytes 2097152 | tf_op jit(solution)/shard_map/stack | solution.py:39
  218.5 2.8 copy.135
  221.3 4.6 %all-to-all-start.2 = ((bf16[16,2,32,512]{3,2,1,0:T(8,128)(2,1)}), bf16[16,2,32,512]{3,2,1,0:T(8,128)(2,1)}, u32[]{:S(2)}, u32[]{:S(2)}) async-start(bf16[16,2,32,512]{3,2,1,0:T(8,128)(2,1)} %copy.135), calls=%async_computation.2 | async-start | bytes 2097152 | tf_op jit(solution)/shard_map/all_to_all | solution.py:40
  228.7 23.9 %all-to-all-done.2 = bf16[16,2,32,512]{3,2,1,0:T(8,128)(2,1)} async-done(((bf16[16,2,32,512]{3,2,1,0:T(8,128)(2,1)}), bf16[16,2,32,512]{3,2,1,0:T(8,128)(2,1)}, u32[]{:S(2)}, u32[]{:S(2)}) %all-to-all-start.2) | async-done | bytes 1048608 | tf_op jit(solution)/shard_map/all_to_all | solution.py:40
  256.7 2.9 %reshape.110 = f32[2,32,8192]{2,1,0:T(8,128)} reshape(f32[1,2,32,16,512]{4,3,2,1,0:T(8,128)} %copy.136) | data formatting | bytes 4194304 | tf_op jit(solution)/shard_map/convert_element_type | solution.py:41
  259.6 3.5 %fusion.49 = bf16[1,2,32,8192]{3,2,1,0:T(8,128)(2,1)} fusion(f32[2,32,8192]{2,1,0:T(8,128)} %reshape.110, bf16[1,2,32,8192]{3,2,1,0:T(8,128)(2,1)S(1)} %copy-done.2, f32[2,32,8192]{2,1,0:T(8,128)S(1)} %bitcast.146, bf16[2,32,8192]{2,1,0:T(8,128)(2,1)} %param.11, f32[2,32]{1,0:T(2,128)S(1)} %broadcast_multiply_fusion, f32[8192]{0:T(1024)S(1)} %bitcast.152, ...), kind=kLoop, calls=%fused_computation.80 | loop fusion | flops 5242880 | bytes 7373312 | tf_op jit(solution)/shard_map/broadcast_in_dim | solution.py:94
  263.1 4.9 %convolution_bitcast_fusion = f32[4,2048,512]{2,1,0:T(8,128)S(1)} fusion(bf16[4,4,2,32,2048]{4,3,2,1,0:T(8,128)(2,1)} %bitcast.154, bf16[2,4,4,32,512]{4,3,2,1,0:T(8,128)(2,1)} %bitcast.155), kind=kOutput, calls=%fused_computation | convolution fusion | flops 2147483648 | bytes 22020096 | tf_op jit(solution)/shard_map/tpmid,mptik->pdk/dot_general | solution.py:84
  268.0 10.4 %fusion.39 = (bf16[2048,512]{1,0:T(8,128)(2,1)S(1)}, bf16[2048,512]{1,0:T(8,128)(2,1)S(1)}, bf16[2048,512]{1,0:T(8,128)(2,1)S(1)}, bf16[2048,512]{1,0:T(8,128)(2,1)S(1)}) fusion(f32[4,2048,512]{2,1,0:T(8,128)S(1)} %convolution_bitcast_fusion, s32[]{:T(128)S(6)} %mul.216, s32[]{:T(128)} %bitcast.37, s32[]{:T(128)} %bitcast.36, s32[2048]{0:T(1024)S(1)} %multiply_add_fusion), kind=kLoop, calls=%fused_computation.59 | loop fusion | flops 75497472 | bytes 25174028 | tf_op jit(solution)/shard_map/convert_element_type | solution.py:25
  278.4 3.2 %add_bitcast_fusion = f32[1,2048,512]{2,1,0:T(8,128)} fusion(bf16[2048,512]{1,0:T(8,128)(2,1)S(1)} %get-tuple-element.17, bf16[2048,512]{1,0:T(8,128)(2,1)S(1)} %get-tuple-element.18, bf16[2048,512]{1,0:T(8,128)(2,1)S(1)} %get-tuple-element.19, bf16[2048,512]{1,0:T(8,128)(2,1)S(1)} %get-tuple-element.16), kind=kLoop, calls=%fused_computation.54 | loop fusion | flops 7340032 | bytes 12582912 | tf_op jit(solution)/shard_map/broadcast_in_dim | solution.py:94
  (61 shorter events, 29.2 us)
Async XLA Ops:
  7.2 31.0 %copy-start = (bf16[1,2048,512]{2,1,0:T(8,128)(2,1)S(1)}, bf16[1,2048,512]{2,1,0:T(8,128)(2,1)}, u32[]{:S(2)}) copy-start(bf16[1,2048,512]{2,1,0:T(8,128)(2,1)} %param.9) | copy-start | bytes 6291460
  7.2 31.0 %all-gather.5.cloned.1.call-start = ((), (), s32[]{:S(2)}) async-start(), calls=%async_computation.4 | async-start | bytes 1310720 | tf_op jit(solution)/shard_map/all_gather | solution.py:62
  44.1 7.6 %copy-start.7 = (bf16[1,8192]{1,0:T(2,128)(2,1)S(1)}, bf16[1,8192]{1,0:T(2,128)(2,1)}, u32[]{:S(2)}) copy-start(bf16[1,8192]{1,0:T(2,128)(2,1)} %param.10) | copy-start | bytes 49156
  44.1 7.8 %copy-start.2 = (bf16[1,2,32,8192]{3,2,1,0:T(8,128)(2,1)S(1)}, bf16[1,2,32,8192]{3,2,1,0:T(8,128)(2,1)}, u32[]{:S(2)}) copy-start(bf16[1,2,32,8192]{3,2,1,0:T(8,128)(2,1)} %param.7) | copy-start | bytes 3145732
  44.1 57.9 %all-to-all-start = ((bf16[16,2,32,2048]{3,2,1,0:T(8,128)(2,1)}), bf16[16,2,32,2048]{3,2,1,0:T(8,128)(2,1)}, u32[]{:S(2)}, u32[]{:S(2)}) async-start(bf16[16,2,32,2048]{3,2,1,0:T(8,128)(2,1)} %bitcast.145), calls=%async_computation | async-start | bytes 8388608 | tf_op jit(solution)/shard_map/all_to_all | solution.py:67
  51.8 68.8 %copy-start.5 = (f32[1,8192]{1,0:T(1,128)}, f32[1,8192]{1,0:T(1,128)S(1)}, u32[]{:S(2)}) copy-start(f32[1,8192]{1,0:T(1,128)S(1)} %convert_element_type.151) | copy-start | bytes 98308
  102.0 3.4 %copy-start.4 = (f32[2,32,4,2048]{3,2,1,0:T(4,128)S(1)}, f32[2,32,4,2048]{3,2,1,0:T(4,128)}, u32[]{:S(2)}) copy-start(f32[2,32,4,2048]{3,2,1,0:T(4,128)} %reshape.107) | copy-start | bytes 6291460
  108.4 34.3 %all-to-all-start.3 = ((bf16[4,2,32,2048]{3,2,1,0:T(8,128)(2,1)}), bf16[4,2,32,2048]{3,2,1,0:T(8,128)(2,1)}, u32[]{:S(2)}, u32[]{:S(2)}) async-start(bf16[4,2,32,2048]{3,2,1,0:T(8,128)(2,1)} %get-tuple-element.20), calls=%async_computation.3 | async-start | bytes 2097152 | tf_op jit(solution)/shard_map/all_to_all | solution.py:81
  142.8 35.1 %all-to-all-start.1 = ((bf16[16,2,16384]{2,1,0:T(2,128)(2,1)}), bf16[16,2,16384]{2,1,0:T(2,128)(2,1)}, u32[]{:S(2)}, u32[]{:S(2)}) async-start(bf16[16,2,16384]{2,1,0:T(2,128)(2,1)} %reshape.147), calls=%async_computation.1 | async-start | bytes 2097152 | tf_op jit(solution)/shard_map/all_to_all | solution.py:31
  150.0 113.2 %all-gather.7.cloned.1.call-start = ((), (), s32[]{:S(2)}) async-start(), calls=%async_computation.5 | async-start | bytes 5242880 | tf_op jit(solution)/shard_map/all_gather | solution.py:82
  221.3 31.3 %all-to-all-start.2 = ((bf16[16,2,32,512]{3,2,1,0:T(8,128)(2,1)}), bf16[16,2,32,512]{3,2,1,0:T(8,128)(2,1)}, u32[]{:S(2)}, u32[]{:S(2)}) async-start(bf16[16,2,32,512]{3,2,1,0:T(8,128)(2,1)} %copy.135), calls=%async_computation.2 | async-start | bytes 2097152 | tf_op jit(solution)/shard_map/all_to_all | solution.py:40
  254.1 5.5 %copy-start.6 = (f32[1,8192]{1,0:T(1,128)S(1)}, f32[1,8192]{1,0:T(1,128)}, u32[]{:S(2)}) copy-start(f32[1,8192]{1,0:T(1,128)} %copy-done.5) | copy-start | bytes 98308
  256.7 2.9 %copy-start.3 = (f32[4,2,4,8,2048]{4,3,0,2,1:T(8,128)S(1)}, f32[4,2,4,8,2048]{4,3,0,2,1:T(8,128)}, u32[]{:S(2)}) copy-start(f32[4,2,4,8,2048]{4,3,0,2,1:T(8,128)} %copy.153) | copy-start | bytes 6291460
  278.4 3.2 %copy-start.1 = (bf16[1,2048,512]{2,1,0:T(8,128)(2,1)S(1)}, bf16[1,2048,512]{2,1,0:T(8,128)(2,1)}, u32[]{:S(2)}) copy-start(bf16[1,2048,512]{2,1,0:T(8,128)(2,1)} %param.9) | copy-start | bytes 6291460
Sparse Core Ops, SparseCore 0:
  9.8 28.3 all-gather.4
  152.6 46.6 all-gather.6
where the time goes:
time: 290 us; the launch traced here: 288 us
  waiting for transfers between devices  130 us (45%)
  local copies, waits for them, and re-layouts  80.4 us (28%)
  other arithmetic  28.9 us (10%)
  starting transfers between devices  25.5 us (9%)
  between operations  15.6 us (5%)
  matrix products  8.46 us (3%)
    all_to_all x1, waiting for transfers between devices, shards(): got = lax.all_to_all(part, ('dp', 'tensor'), 0, 0, tiled=True)  47.1 us
    all_gather x1, waiting for transfers between devices, shards(): cotan_all = lax.all_gather(cotan, 'dp', axis=1, tiled=True)  30.3 us
    all_to_all x1, waiting for transfers between devices, later_sum(): lax.all_to_all(branch_path.astype(jnp.bfloat16)[None], 'section', 3, 0, t...  27.2 us
    all_to_all x1, waiting for transfers between devices, later_sum(): back = lax.all_to_all(stacked, 'section', 0, 3, tiled=True)  23.9 us
    unnamed x20, local copies, waits for them, and re-layouts  21.6 us
    another operation x3, local copies, waits for them, and re-layouts, later_sum(): stacked = jnp.stack(outs).astype(jnp.bfloat16)  11 us
    convert_element_type x1, other arithmetic, dither(): moved.astype(jnp.bfloat16)  10.4 us
    another operation x14, local copies, waits for them, and re-layouts  9.33 us
  transfers between devices with their start and end apart: 6, of which 4 were waited for; matrix products, arithmetic and copies ran while one was open for 30% of the time, Pallas kernels for 0%

commit v1 on v0

--- a/solution.py
+++ b/solution.py
@@ -59,7 +59,25 @@
     centered_input = input_float * inverse_scale
     gain_float = norm_gain[0].astype(jnp.float32)
     normed_values = (centered_input * gain_float).astype(jnp.bfloat16)
-    cotan_all = lax.all_gather(cotan, "dp", axis=1, tiled=True)
+
+    def apply_copies(mat, shard_axis="dp"):
+        extent = lax.axis_size(shard_axis)
+        entries = tuple(((b, (b + 1) % extent) for b in range(extent)))
+        panels = tuple(((b, (b - 1) % extent) for b in range(extent)))
+        d_next, view_out = ([mat], [mat])
+        for _ in range(extent // 2):
+            d_next.append(lax.ppermute(d_next[-1], shard_axis, entries))
+        i0 = 0
+        while i0 < (extent - 1) // 2:
+            view_out.append(lax.ppermute(view_out[-1], shard_axis, panels))
+            i0 = i0 + 1
+        return jnp.roll(
+            jnp.concatenate([*d_next[::-1], *view_out[1:]], axis=1),
+            shift=(lax.axis_index(shard_axis) - extent // 2) * mat.shape[1],
+            axis=1,
+        )
+
+    cotan_all = apply_copies(cotan)
     part = jnp.einsum("mtk,dk->mtd", cotan_all, weight, preferred_element_type=jnp.float32).astype(
         jnp.bfloat16
     )

time: 290 us -> 279 us (0.962)
  waiting for transfers between devices: 130 us -> 111 us
  starting transfers between devices: 25.5 us -> 31.6 us
    all_gather x1 -> x0, waiting for transfers between devices: 30.3 us -> none  [shards(): cotan_all = lax.all_gather(cotan, 'dp', axis=1, tiled=True)]
    ppermute x0 -> x3, waiting for transfers between devices: none -> 12.3 us  [the longest x2 11.7 us: apply_copies(): d_next.append(lax.ppermute(d_next[-1], shard_axis, entries))]
    ppermute x0 -> x3, starting transfers between devices: none -> 3.68 us  [the longest x2 3.23 us: apply_copies(): d_next.append(lax.ppermute(d_next[-1], shard_axis, entries))]
    unnamed x20 -> x29, local copies, waits for them, and re-layouts: 21.6 us -> 23.6 us
  transfers between devices with their start and end apart: 6 -> 8, of which waited for: 4 -> 6; matrix products, arithmetic and copies ran while one was open for 30% -> 32% of each run, Pallas kernels for 0% -> 0%
where the time goes in v1:
time: 279 us; the launch traced here: 277 us
  waiting for transfers between devices  111 us (40%)
  local copies, waits for them, and re-layouts  82.3 us (29%)
  starting transfers between devices  31.6 us (11%)
  other arithmetic  28.9 us (10%)
  between operations  15.7 us (6%)
  matrix products  7.24 us (3%)
    all_to_all x1, waiting for transfers between devices, shards(): got = lax.all_to_all(part, ('dp', 'tensor'), 0, 0, tiled=True)  47.1 us
    all_to_all x1, waiting for transfers between devices, later_sum(): lax.all_to_all(branch_path.astype(jnp.bfloat16)[None], 'section', 3, 0, t...  27.2 us
    all_to_all x1, waiting for transfers between devices, later_sum(): back = lax.all_to_all(stacked, 'section', 0, 3, tiled=True)  23.9 us
    unnamed x29, local copies, waits for them, and re-layouts  23.6 us
    ppermute x2, waiting for transfers between devices, apply_copies(): d_next.append(lax.ppermute(d_next[-1], shard_axis, entries))  11.7 us
    another operation x3, local copies, waits for them, and re-layouts, later_sum(): stacked = jnp.stack(outs).astype(jnp.bfloat16)  11 us
    convert_element_type x1, other arithmetic, dither(): moved.astype(jnp.bfloat16)  10.4 us
    another operation x14, local copies, waits for them, and re-layouts  9.21 us
  transfers between devices with their start and end apart: 8, of which 6 were waited for; matrix products, arithmetic and copies ran while one was open for 32% of the time, Pallas kernels for 0%

profile of v1, /device:TPU:8, one launch (start us, length us, event | category | flops | bytes accessed | tf_op | source)
XLA Modules:
  0.0 276.7 jit_solution(3206488395415982483)
XLA Ops:
  8.8 6.7 %collective-permute-done = bf16[2,128,512]{2,1,0:T(8,128)(2,1)S(1)} collective-permute-done((bf16[2,128,512]{2,1,0:T(8,128)(2,1)}, bf16[2,128,512]{2,1,0:T(8,128)(2,1)S(1)}, u32[]{:S(2)}, u32[]{:S(2)}) %collective-permute-start) | collective-permute-done | bytes 262176 | tf_op jit(solution)/shard_map/ppermute | solution.py:69
  17.5 5.0 %collective-permute-done.1 = bf16[2,128,512]{2,1,0:T(8,128)(2,1)S(1)} collective-permute-done((bf16[2,128,512]{2,1,0:T(8,128)(2,1)S(1)}, bf16[2,128,512]{2,1,0:T(8,128)(2,1)S(1)}, u32[]{:S(2)}, u32[]{:S(2)}) %collective-permute-start.1) | collective-permute-done | bytes 262176 | tf_op jit(solution)/shard_map/ppermute | solution.py:69
  30.1 8.5 %all-to-all-start = ((bf16[16,2,32,2048]{3,2,1,0:T(8,128)(2,1)}), bf16[16,2,32,2048]{3,2,1,0:T(8,128)(2,1)}, u32[]{:S(2)}, u32[]{:S(2)}) async-start(bf16[16,2,32,2048]{3,2,1,0:T(8,128)(2,1)} %bitcast.146), calls=%async_computation | async-start | bytes 8388608 | tf_op jit(solution)/shard_map/all_to_all | solution.py:85
  41.8 47.1 %all-to-all-done = bf16[16,2,32,2048]{3,2,1,0:T(8,128)(2,1)} async-done(((bf16[16,2,32,2048]{3,2,1,0:T(8,128)(2,1)}), bf16[16,2,32,2048]{3,2,1,0:T(8,128)(2,1)}, u32[]{:S(2)}, u32[]{:S(2)}) %all-to-all-start) | async-done | bytes 4194336 | tf_op jit(solution)/shard_map/all_to_all | solution.py:85
  88.9 3.4 %bitcast_convert_fusion = f32[4,4,2,32,2048]{4,3,2,1,0:T(8,128)S(1)} fusion(bf16[16,2,32,2048]{3,2,1,0:T(8,128)(2,1)} %all-to-all-done), kind=kLoop, calls=%fused_computation.129 | loop fusion | flops 2097152 | bytes 12582912 | tf_op jit(solution)/shard_map/convert_element_type | solution.py:86
  92.3 3.0 %multiply_reduce_fusion = (f32[2,32]{1,0:T(2,128)S(1)}, f32[4,1,2,32,2048]{4,3,2,1,0:T(8,128)S(1)}, bf16[4,2,32,2048]{3,2,1,0:T(8,128)(2,1)}) fusion(f32[2,32,4,2048]{3,2,1,0:T(4,128)S(1)} %copy-done.4, f32[2,32]{1,0:T(2,128)S(1)} %add_rsqrt_fusion, f32[4,2048]{1,0:T(4,128)S(1)} %reshape.106, f32[4,4,2,32,2048]{4,3,2,1,0:T(8,128)S(1)} %bitcast_convert_fusion), kind=kLoop, calls=%fused_computation.78 | loop fusion | flops 4718528 | bytes 13664768 | tf_op jit(solution)/shard_map/reduce_sum | solution.py:94
  95.3 5.9 %all-to-all-start.3 = ((bf16[4,2,32,2048]{3,2,1,0:T(8,128)(2,1)}), bf16[4,2,32,2048]{3,2,1,0:T(8,128)(2,1)}, u32[]{:S(2)}, u32[]{:S(2)}) async-start(bf16[4,2,32,2048]{3,2,1,0:T(8,128)(2,1)} %get-tuple-element.20), calls=%async_computation.3 | async-start | bytes 2097152 | tf_op jit(solution)/shard_map/all_to_all | solution.py:99
  103.8 3.6 %reshape.101 = f32[1,2,32,8192]{3,2,1,0:T(8,128)} reshape(f32[2,32,4,2048]{3,2,1,0:T(4,128)} %copy.101) | data formatting | bytes 4194304 | tf_op jit(solution)/shard_map/reshape | solution.py:90
  107.5 3.1 %multiply_convert_fusion.1 = bf16[1,2,32,8192]{3,2,1,0:T(8,128)(2,1)} fusion(f32[1,2,32,8192]{3,2,1,0:T(8,128)} %reshape.101, bf16[1,2,32,8192]{3,2,1,0:T(8,128)(2,1)S(1)} %copy-done.2, f32[2,32]{1,0:T(2,128)S(1)} %broadcast_multiply_fusion, f32[8192]{0:T(1024)S(1)} %bitcast.155, f32[2,32]{1,0:T(2,128)S(1)} %add_rsqrt_fusion), kind=kLoop, calls=%fused_computation.77 | loop fusion | flops 3670016 | bytes 4227584 | tf_op jit(solution)/shard_map/convert_element_type | solution.py:32
  110.6 9.2 %copy.104 = bf16[1,2,32,8192]{2,1,0,3:T(2,128)(2,1)} copy(bf16[1,2,32,8192]{3,2,1,0:T(8,128)(2,1)} %multiply_convert_fusion.1) | data formatting | bytes 2097152 | tf_op jit(solution)/shard_map/convert_element_type | solution.py:32
  119.7 9.9 %reshape.145 = bf16[16,2,16384]{2,1,0:T(2,128)(2,1)} reshape(bf16[8192,1,2,32]{3,2,1,0:T(2,128)(2,1)} %bitcast.144) | data formatting | bytes 2097152
  129.6 8.6 %all-to-all-start.1 = ((bf16[16,2,16384]{2,1,0:T(2,128)(2,1)}), bf16[16,2,16384]{2,1,0:T(2,128)(2,1)}, u32[]{:S(2)}, u32[]{:S(2)}) async-start(bf16[16,2,16384]{2,1,0:T(2,128)(2,1)} %reshape.145), calls=%async_computation.1 | async-start | bytes 2097152 | tf_op jit(solution)/shard_map/all_to_all | solution.py:31
  139.0 27.2 %all-to-all-done.1 = bf16[16,2,16384]{2,1,0:T(2,128)(2,1)} async-done(((bf16[16,2,16384]{2,1,0:T(2,128)(2,1)}), bf16[16,2,16384]{2,1,0:T(2,128)(2,1)}, u32[]{:S(2)}, u32[]{:S(2)}) %all-to-all-start.1) | async-done | bytes 1048608 | tf_op jit(solution)/shard_map/all_to_all | solution.py:31
  166.3 10.0 %reshape.146 = bf16[8192,1,2,32]{3,2,1,0:T(2,128)(2,1)} reshape(bf16[16,2,16384]{2,1,0:T(2,128)(2,1)} %all-to-all-done.1) | data formatting | bytes 2097152
  176.3 9.0 %copy.105 = bf16[1,2,32,8192]{3,2,1,0:T(8,128)(2,1)} copy(bf16[1,2,32,8192]{2,1,0,3:T(2,128)(2,1)} %bitcast.145) | data formatting | bytes 2097152 | tf_op jit(solution)/shard_map/all_to_all | solution.py:31
  199.2 7.5 %stack.3 = bf16[16,2,32,512]{3,0,2,1:T(8,128)(2,1)} concatenate(bf16[1,2,32,512]{3,0,2,1:T(2,128)(2,1)S(1)} %fusion.52, bf16[1,2,32,512]{3,0,2,1:T(2,128)(2,1)S(1)} %copy.121, bf16[1,2,32,512]{3,0,2,1:T(2,128)(2,1)} %copy.122, bf16[1,2,32,512]{3,0,2,1:T(2,128)(2,1)S(1)} %copy.123, bf16[1,2,32,512]{3,0,2,1:T(2,128)(2,1)} %copy.124, bf16[1,2,32,512]{3,0,2,1:T(2,128)(2,1)} %copy.125, ...), dimensions={0} | concatenate | bytes 2097152 | tf_op jit(solution)/shard_map/stack | solution.py:39
  206.7 2.8 %copy.134 = bf16[16,2,32,512]{3,2,1,0:T(8,128)(2,1)} copy(bf16[16,2,32,512]{3,0,2,1:T(8,128)(2,1)} %stack.3) | data formatting | bytes 2097152 | tf_op jit(solution)/shard_map/stack | solution.py:39
  209.5 4.6 %all-to-all-start.2 = ((bf16[16,2,32,512]{3,2,1,0:T(8,128)(2,1)}), bf16[16,2,32,512]{3,2,1,0:T(8,128)(2,1)}, u32[]{:S(2)}, u32[]{:S(2)}) async-start(bf16[16,2,32,512]{3,2,1,0:T(8,128)(2,1)} %copy.134), calls=%async_computation.2 | async-start | bytes 2097152 | tf_op jit(solution)/shard_map/all_to_all | solution.py:40
  217.0 23.9 %all-to-all-done.2 = bf16[16,2,32,512]{3,2,1,0:T(8,128)(2,1)} async-done(((bf16[16,2,32,512]{3,2,1,0:T(8,128)(2,1)}), bf16[16,2,32,512]{3,2,1,0:T(8,128)(2,1)}, u32[]{:S(2)}, u32[]{:S(2)}) %all-to-all-start.2) | async-done | bytes 1048608 | tf_op jit(solution)/shard_map/all_to_all | solution.py:40
  244.9 2.9 %reshape.110 = f32[2,32,8192]{2,1,0:T(8,128)} reshape(f32[1,2,32,16,512]{4,3,2,1,0:T(8,128)} %copy.135) | data formatting | bytes 4194304 | tf_op jit(solution)/shard_map/convert_element_type | solution.py:41
  247.8 3.5 %fusion.49 = bf16[1,2,32,8192]{3,2,1,0:T(8,128)(2,1)} fusion(f32[2,32,8192]{2,1,0:T(8,128)} %reshape.110, bf16[1,2,32,8192]{3,2,1,0:T(8,128)(2,1)S(1)} %copy-done.2, f32[2,32,8192]{2,1,0:T(8,128)S(1)} %bitcast.147, bf16[2,32,8192]{2,1,0:T(8,128)(2,1)} %param.11, f32[2,32]{1,0:T(2,128)S(1)} %broadcast_multiply_fusion, f32[8192]{0:T(1024)S(1)} %bitcast.156, ...), kind=kLoop, calls=%fused_computation.80 | loop fusion | flops 5242880 | bytes 7373312 | tf_op jit(solution)/shard_map/broadcast_in_dim | solution.py:112
  251.4 4.9 %convolution_bitcast_fusion = f32[4,2048,512]{2,1,0:T(8,128)S(1)} fusion(bf16[4,4,2,32,2048]{4,3,2,1,0:T(8,128)(2,1)} %bitcast.158, bf16[2,4,4,32,512]{4,3,2,1,0:T(8,128)(2,1)} %bitcast.152), kind=kOutput, calls=%fused_computation | convolution fusion | flops 2147483648 | bytes 22020096 | tf_op jit(solution)/shard_map/tpmid,mptik->pdk/dot_general | solution.py:102
  256.2 10.4 %fusion.39 = (bf16[2048,512]{1,0:T(8,128)(2,1)S(1)}, bf16[2048,512]{1,0:T(8,128)(2,1)S(1)}, bf16[2048,512]{1,0:T(8,128)(2,1)S(1)}, bf16[2048,512]{1,0:T(8,128)(2,1)S(1)}) fusion(f32[4,2048,512]{2,1,0:T(8,128)S(1)} %convolution_bitcast_fusion, s32[]{:T(128)S(6)} %mul.220, s32[]{:T(128)} %bitcast.37, s32[]{:T(128)} %bitcast.36, s32[2048]{0:T(1024)S(1)} %multiply_add_fusion), kind=kLoop, calls=%fused_computation.59 | loop fusion | flops 75497472 | bytes 25174028 | tf_op jit(solution)/shard_map/convert_element_type | solution.py:25
  266.7 3.2 %add_bitcast_fusion = f32[1,2048,512]{2,1,0:T(8,128)} fusion(bf16[2048,512]{1,0:T(8,128)(2,1)S(1)} %get-tuple-element.17, bf16[2048,512]{1,0:T(8,128)(2,1)S(1)} %get-tuple-element.18, bf16[2048,512]{1,0:T(8,128)(2,1)S(1)} %get-tuple-element.19, bf16[2048,512]{1,0:T(8,128)(2,1)S(1)} %get-tuple-element.16), kind=kLoop, calls=%fused_computation.54 | loop fusion | flops 7340032 | bytes 12582912 | tf_op jit(solution)/shard_map/broadcast_in_dim | solution.py:112
  (75 shorter events, 37.1 us)
Async XLA Ops:
  7.2 18.2 %copy-start = (bf16[1,2048,512]{2,1,0:T(8,128)(2,1)S(1)}, bf16[1,2048,512]{2,1,0:T(8,128)(2,1)}, u32[]{:S(2)}) copy-start(bf16[1,2048,512]{2,1,0:T(8,128)(2,1)} %param.9) | copy-start | bytes 6291460
  7.2 8.3 %collective-permute-start = (bf16[2,128,512]{2,1,0:T(8,128)(2,1)}, bf16[2,128,512]{2,1,0:T(8,128)(2,1)S(1)}, u32[]{:S(2)}, u32[]{:S(2)}) collective-permute-start(bf16[2,128,512]{2,1,0:T(8,128)(2,1)} %bitcast.153), channel_id=1, source_target_pairs={{0,64},{64,128},{128,192},{192,0},{1,65},{65,129},{129,193},{193,1... | collective-permute-start | bytes 786440 | tf_op jit(solution)/shard_map/ppermute | solution.py:69
  15.5 7.0 %collective-permute-start.1 = (bf16[2,128,512]{2,1,0:T(8,128)(2,1)S(1)}, bf16[2,128,512]{2,1,0:T(8,128)(2,1)S(1)}, u32[]{:S(2)}, u32[]{:S(2)}) collective-permute-start(bf16[2,128,512]{2,1,0:T(8,128)(2,1)S(1)} %collective-permute-done), channel_id=1, source_target_pairs={{0,64},{64,128},{128,192},{192,0},{1,65},{65,129},{129,193},{193,1... | collective-permute-start | bytes 786440 | tf_op jit(solution)/shard_map/ppermute | solution.py:69
  17.1 7.1 %collective-permute-start.2 = (bf16[2,128,512]{2,1,0:T(8,128)(2,1)}, bf16[2,128,512]{2,1,0:T(8,128)(2,1)S(1)}, u32[]{:S(2)}, u32[]{:S(2)}) collective-permute-start(bf16[2,128,512]{2,1,0:T(8,128)(2,1)} %bitcast.154), channel_id=1, source_target_pairs={{0,192},{64,0},{128,64},{192,128},{1,193},{65,1},{129,65},{193,129... | collective-permute-start | bytes 786440 | tf_op jit(solution)/shard_map/ppermute | solution.py:72
  25.4 2.4 copy-start.5
  30.1 8.6 %copy-start.8 = (bf16[1,8192]{1,0:T(2,128)(2,1)S(1)}, bf16[1,8192]{1,0:T(2,128)(2,1)}, u32[]{:S(2)}) copy-start(bf16[1,8192]{1,0:T(2,128)(2,1)} %param.10) | copy-start | bytes 49156
  30.1 8.7 %copy-start.2 = (bf16[1,2,32,8192]{3,2,1,0:T(8,128)(2,1)S(1)}, bf16[1,2,32,8192]{3,2,1,0:T(8,128)(2,1)}, u32[]{:S(2)}) copy-start(bf16[1,2,32,8192]{3,2,1,0:T(8,128)(2,1)} %param.7) | copy-start | bytes 3145732
  30.1 58.8 %all-to-all-start = ((bf16[16,2,32,2048]{3,2,1,0:T(8,128)(2,1)}), bf16[16,2,32,2048]{3,2,1,0:T(8,128)(2,1)}, u32[]{:S(2)}, u32[]{:S(2)}) async-start(bf16[16,2,32,2048]{3,2,1,0:T(8,128)(2,1)} %bitcast.146), calls=%async_computation | async-start | bytes 8388608 | tf_op jit(solution)/shard_map/all_to_all | solution.py:85
  38.7 68.8 %copy-start.6 = (f32[1,8192]{1,0:T(1,128)}, f32[1,8192]{1,0:T(1,128)S(1)}, u32[]{:S(2)}) copy-start(f32[1,8192]{1,0:T(1,128)S(1)} %convert_element_type.151) | copy-start | bytes 98308
  88.9 3.4 %copy-start.4 = (f32[2,32,4,2048]{3,2,1,0:T(4,128)S(1)}, f32[2,32,4,2048]{3,2,1,0:T(4,128)}, u32[]{:S(2)}) copy-start(f32[2,32,4,2048]{3,2,1,0:T(4,128)} %reshape.107) | copy-start | bytes 6291460
  95.3 34.3 %all-to-all-start.3 = ((bf16[4,2,32,2048]{3,2,1,0:T(8,128)(2,1)}), bf16[4,2,32,2048]{3,2,1,0:T(8,128)(2,1)}, u32[]{:S(2)}, u32[]{:S(2)}) async-start(bf16[4,2,32,2048]{3,2,1,0:T(8,128)(2,1)} %get-tuple-element.20), calls=%async_computation.3 | async-start | bytes 2097152 | tf_op jit(solution)/shard_map/all_to_all | solution.py:99
  129.6 36.6 %all-to-all-start.1 = ((bf16[16,2,16384]{2,1,0:T(2,128)(2,1)}), bf16[16,2,16384]{2,1,0:T(2,128)(2,1)}, u32[]{:S(2)}, u32[]{:S(2)}) async-start(bf16[16,2,16384]{2,1,0:T(2,128)(2,1)} %reshape.145), calls=%async_computation.1 | async-start | bytes 2097152 | tf_op jit(solution)/shard_map/all_to_all | solution.py:31
  138.3 113.1 %all-gather.3.cloned.1.call-start = ((), (), s32[]{:S(2)}) async-start(), calls=%async_computation.4 | async-start | bytes 5242880 | tf_op jit(solution)/shard_map/all_gather | solution.py:100
  209.5 31.3 %all-to-all-start.2 = ((bf16[16,2,32,512]{3,2,1,0:T(8,128)(2,1)}), bf16[16,2,32,512]{3,2,1,0:T(8,128)(2,1)}, u32[]{:S(2)}, u32[]{:S(2)}) async-start(bf16[16,2,32,512]{3,2,1,0:T(8,128)(2,1)} %copy.134), calls=%async_computation.2 | async-start | bytes 2097152 | tf_op jit(solution)/shard_map/all_to_all | solution.py:40
  242.3 5.5 %copy-start.7 = (f32[1,8192]{1,0:T(1,128)S(1)}, f32[1,8192]{1,0:T(1,128)}, u32[]{:S(2)}) copy-start(f32[1,8192]{1,0:T(1,128)} %copy-done.6) | copy-start | bytes 98308
  244.9 2.9 %copy-start.3 = (f32[4,2,4,8,2048]{4,3,0,2,1:T(8,128)S(1)}, f32[4,2,4,8,2048]{4,3,0,2,1:T(8,128)}, u32[]{:S(2)}) copy-start(f32[4,2,4,8,2048]{4,3,0,2,1:T(8,128)} %copy.152) | copy-start | bytes 6291460
  266.6 3.2 %copy-start.1 = (bf16[1,2048,512]{2,1,0:T(8,128)(2,1)S(1)}, bf16[1,2048,512]{2,1,0:T(8,128)(2,1)}, u32[]{:S(2)}) copy-start(bf16[1,2048,512]{2,1,0:T(8,128)(2,1)} %param.9) | copy-start | bytes 6291460
Sparse Core Ops, SparseCore 0:
  140.9 46.6 all-gather.2
